TPU v7x, 512 devices: a whole 4x8x8 slice. The times are simulated.
512 devices in a mesh: seq: 64 (over z_hi, y, x), tp: 8 (over z_lo, core).
Axes of the slice: x: 4, y: 8, z: 8 (z_hi: 2, z_lo: 4; z = z_hi * 4 + z_lo), core: 2. Of those that a mesh axis runs over, the one named last changes fastest.
Arguments:
- residual: bfloat16 [16384, 5376], P('seq', 'tp'), may hold values from -10.5 to 10.5
- input_gain: float32 [5376], replicated, may hold values from 0.25 to 1.75
- w_query: bfloat16 [5376, 4096], P('seq', 'tp'), may hold values from -0.078125 to 0.078125
- key_weight: bfloat16 [5376, 2048], P('seq', 'tp'), may hold values from -0.078125 to 0.078125
- value_weight: bfloat16 [5376, 2048], P('seq', 'tp'), may hold values from -0.078125 to 0.078125
- query_gain: float32 [128], replicated, may hold values from 0.25 to 1.75
- key_gain: float32 [128], replicated, may hold values from 0.25 to 1.75
- w_out: bfloat16 [4096, 5376], P('tp', 'seq'), may hold values from -0.1640625 to 0.1640625
- post_gain: float32 [5376], replicated, may hold values from 0.25 to 1.75
- positions: int32 [16384], replicated, may hold values from 0 to 24063, as said below
Outputs:
- mixed: bfloat16 [16384, 5376], P('seq', 'tp')
Inputs may be any that keep to these rules, and one draw needn't show every extreme that they name: positions start at 0 and rise by 1 over the first 1024 tokens; after that they rise by 1 or 2 from each token to the next, by 2 at exactly (15360) // 2 tokens.
All inputs are finite; a program needn't handle non-finite values.
Results may differ from a plain program's by a relative error of at most 0.017.
Values may be sent and summed in bfloat16 or wider, within the bound.
No kernel may reach another device: no remote copies, remote signals or barrier semaphores. Data moves between devices by JAX's collectives and lax.ppermute only.
A program may use at most 128 MiB of HBM per device.

v0:
```python
import jax
import jax.numpy as jnp
from jax import lax
from jax.sharding import PartitionSpec as P

LOOKBACK_SPAN = 1024
epsilon = 1e-06
score_scale = 168.0 ** (-0.5)
rotary_base = 10000.0


def from_behind(block, axis, distance):
    devices = range(lax.axis_size(axis))
    route = [(i - distance, i) for i in devices if i - distance in devices]
    return lax.ppermute(block, axis, route)


def norm_scale(value_matrix, gain):
    mean_square = jnp.mean(value_matrix * value_matrix, axis=-1, keepdims=True)
    return value_matrix * lax.rsqrt(mean_square + epsilon) * gain


def rotary(value_matrix, places):
    half_dim = value_matrix.shape[-1] // 2
    inverse = rotary_base ** (-jnp.arange(half_dim, dtype=jnp.float32) / half_dim)
    angles = places.astype(jnp.float32)[:, None] * inverse[None, :]
    cosine = jnp.cos(angles)[:, None, :]
    sine = jnp.sin(angles)[:, None, :]
    first = value_matrix[..., :half_dim]
    second = value_matrix[..., half_dim:]
    return jnp.concatenate(
        [first * cosine - second * sine, second * cosine + first * sine], axis=-1
    )


def local(
    residual,
    input_gain,
    w_query,
    key_weight,
    value_weight,
    query_gain,
    key_gain,
    w_out,
    post_gain,
    positions,
):
    tok_rows = residual.shape[0]
    seq_at = lax.axis_index("seq")
    tp_at = lax.axis_index("tp")
    head_dim = query_gain.shape[0]
    local_kv = key_weight.shape[1] // head_dim
    query_group = w_query.shape[1] // key_weight.shape[1]
    gathered = lax.all_gather(residual, "tp", axis=1, tiled=True)
    normalized_input = norm_scale(gathered.astype(jnp.float32), input_gain).astype(jnp.bfloat16)
    own_places = lax.dynamic_slice_in_dim(positions, seq_at * tok_rows, tok_rows, 0)
    reach = (LOOKBACK_SPAN - 2) // tok_rows + 1

    def attend(query_matrix, stacked, key_places, valid):
        key_matrix = stacked[0].reshape(-1, local_kv, head_dim)
        value_matrix = stacked[1].reshape(-1, local_kv, head_dim)
        scores = (
            jnp.einsum(
                "qkgd,skd->kgqs", query_matrix, key_matrix, preferred_element_type=jnp.float32
            )
            * score_scale
        )
        distance = own_places[:, None] - key_places[None, :]
        allowed = valid[None, :] & (distance >= 0) & (distance < LOOKBACK_SPAN)
        weights = jnp.where(allowed[None, None], jnp.exp(scores), jnp.zeros_like(scores))
        total = jnp.sum(weights, axis=-1)
        summed = jnp.einsum(
            "kgqs,skd->qkgd",
            weights.astype(jnp.bfloat16),
            value_matrix,
            preferred_element_type=jnp.float32,
        )
        return (total, summed)

    pieces = (
        lax.all_gather(w_query, "seq", axis=0, tiled=True),
        lax.all_gather(key_weight, "seq", axis=0, tiled=True),
        lax.all_gather(value_weight, "seq", axis=0, tiled=True),
    )
    queries_raw, unrotated_keys, projected_values = tuple(
        (jnp.dot(normalized_input, piece, preferred_element_type=jnp.float32) for piece in pieces)
    )
    key_matrix = rotary(
        norm_scale(unrotated_keys.reshape(tok_rows, local_kv, head_dim), key_gain), own_places
    )
    stacked = jnp.stack(
        [key_matrix.reshape(tok_rows, local_kv * head_dim), projected_values]
    ).astype(jnp.bfloat16)
    pieces = []
    for distance in range(reach, 0, -1):
        pieces.append(from_behind(stacked, "seq", distance))
    halo = jnp.concatenate(pieces, axis=1)
    query_matrix = rotary(
        norm_scale(queries_raw.reshape(tok_rows, local_kv * query_group, head_dim), query_gain),
        own_places,
    )
    query_matrix = query_matrix.astype(jnp.bfloat16).reshape(
        tok_rows, local_kv, query_group, head_dim
    )
    inner_total, inner_sum = attend(
        query_matrix, stacked, own_places, jnp.ones((tok_rows,), jnp.bool_)
    )
    span = halo.shape[1]
    padded_places = jnp.concatenate([jnp.zeros((span,), jnp.int32), positions])
    halo_places = lax.dynamic_slice_in_dim(padded_places, seq_at * tok_rows, span, 0)
    halo_valid = seq_at * tok_rows - span + jnp.arange(span, dtype=jnp.int32) >= 0
    outer_total, outer_sum = attend(query_matrix, halo, halo_places, halo_valid)
    total = jnp.transpose(inner_total + outer_total, (2, 0, 1))
    merged = (inner_sum + outer_sum) / total[..., None]
    attended = merged.astype(jnp.bfloat16).reshape(tok_rows, local_kv * query_group * head_dim)
    partial_out = jnp.dot(
        attended,
        lax.all_gather(w_out, "seq", axis=1, tiled=True),
        preferred_element_type=jnp.float32,
    )
    summed_cols = lax.psum_scatter(
        partial_out.astype(jnp.bfloat16), "tp", scatter_dimension=1, tiled=True
    ).astype(jnp.float32)
    full_width = post_gain.shape[0]
    squares = lax.psum(jnp.sum(summed_cols * summed_cols, axis=1), "tp")
    inverse_rms = lax.rsqrt(squares / full_width + epsilon)
    gain_part = lax.dynamic_slice_in_dim(
        post_gain, tp_at * summed_cols.shape[1], summed_cols.shape[1], 0
    )
    return (residual.astype(jnp.float32) + summed_cols * inverse_rms[:, None] * gain_part).astype(
        jnp.bfloat16
    )


def solution(mesh):
    in_specs = (
        P("seq", "tp"),
        P(),
        P("seq", "tp"),
        P("seq", "tp"),
        P("seq", "tp"),
        P(),
        P(),
        P("tp", "seq"),
        P(),
        P(),
    )
    out_specs = P("seq", "tp")
    return jax.shard_map(local, mesh=mesh, in_specs=in_specs, out_specs=out_specs, check_vma=False)
```

profile of v0, /device:TPU:8, one launch (start us, length us, event | category | flops | bytes accessed | tf_op | source)
XLA Modules:
  0.0 810.8 jit_solution(6384950764701939511)
XLA Ops:
  6.5 0.0 all-gather.10.cloned.1.call-start
  6.5 0.7 all-gather.10.cloned.1.call-update
  7.3 0.0 all-gather.14.cloned.1.call-start
  7.3 0.7 all-gather.14.cloned.1.call-update
  8.0 0.0 all-gather.12.cloned.1.call-start
  8.1 0.7 all-gather.12.cloned.1.call-update
  8.7 0.0 all-gather.16.cloned.1.call-start
  8.8 0.5 all-gather.16.cloned.1.call-update
  9.3 0.0 all-gather.18.cloned.1.call-start
  9.4 0.5 all-gather.18.cloned.1.call-update
  9.9 0.0 reduce-scatter.2.cloned.1.call-start
  10.0 0.8 fusion.45
  10.8 0.8 pad_dynamic-slice_fusion
  11.5 0.5 multiply_cosine_fusion
  12.1 0.0 copy-start.9
  12.1 46.5 %all-gather.10.cloned.1.call-done = bf16[256,5376]{0,1:T(8,128)(2,1)} async-done(((bf16[256,672]{0,1:T(8,128)(2,1)}), bf16[256,5376]{0,1:T(8,128)(2,1)}) %all-gather.10.cloned.1.call-update) | async-done | bytes 2752528 | tf_op jit(solution)/shard_map/all_gather | solution.py:54
  58.5 2.7 fusion
  61.2 146.3 %all-gather.14.cloned.1.call-done = bf16[64,84,256]{2,1,0:T(8,128)(2,1)} async-done(((bf16[1,84,256]{2,1,0:T(8,128)(2,1)}), bf16[64,84,256]{2,1,0:T(8,128)(2,1)}) %all-gather.14.cloned.1.call-update) | async-done | bytes 2752528 | tf_op jit(solution)/shard_map/all_gather | solution.py:82
  207.5 5.2 reshape.181
  212.7 0.0 copy-done
  212.7 3.5 multiply_reduce_fusion.1
  216.2 0.1 copy.40
  216.3 0.0 copy-start.10
  216.3 0.8 multiply_multiply_fusion.1
  217.1 0.2 subtract_convert_fusion.1
  217.3 0.1 pad_maximum_fusion.2
  217.4 0.1 copy.46
  217.5 134.0 %all-gather.12.cloned.1.call-done = bf16[64,84,256]{2,1,0:T(8,128)(2,1)} async-done(((bf16[1,84,256]{2,1,0:T(8,128)(2,1)}), bf16[64,84,256]{2,1,0:T(8,128)(2,1)}) %all-gather.12.cloned.1.call-update) | async-done | bytes 2752528 | tf_op jit(solution)/shard_map/all_gather | solution.py:83
  351.5 5.2 reshape.179
  356.7 0.0 copy-done.6
  356.7 3.5 convolution_convert_fusion.1
  360.2 3.4 collective-permute-start
  363.6 0.8 fusion.20
  364.4 4.7 collective-permute-start.1
  369.0 3.6 collective-permute-start.2
  372.7 0.8 fusion.33
  373.5 2.9 collective-permute-start.3
  376.4 0.0 collective-permute-done
  376.4 0.0 collective-permute-done.1
  376.5 7.2 collective-permute-done.2
  383.7 4.6 collective-permute-done.3
  388.3 1.0 fusion.46
  389.4 168.5 %all-gather.16.cloned.1.call-done = bf16[64,84,512]{2,1,0:T(8,128)(2,1)} async-done(((bf16[1,84,512]{2,1,0:T(8,128)(2,1)}), bf16[64,84,512]{2,1,0:T(8,128)(2,1)}) %all-gather.16.cloned.1.call-update) | async-done | bytes 5505040 | tf_op jit(solution)/shard_map/all_gather | solution.py:81
  557.9 8.9 %reshape.183 = bf16[5376,512]{1,0:T(8,128)(2,1)} reshape(bf16[64,84,512]{2,1,0:T(8,128)(2,1)} %all-gather.16.cloned.1.call-done) | data formatting | bytes 11010048
  566.8 6.5 fusion.40
  573.3 1.3 reshape.176
  574.6 0.3 multiply_reduce_fusion
  575.0 0.0 copy-done.8
  575.0 0.3 multiply_multiply_fusion
  575.3 0.5 subtract_convert_fusion
  575.9 0.0 copy-done.4
  576.0 0.5 fusion.47
  576.5 1.3 fusion.3
  577.8 0.2 fusion.31
  578.1 1.0 fusion.24
  579.0 151.3 %all-gather.18.cloned.1.call-done = bf16[64,84,512]{2,1,0:T(8,128)(2,1)} async-done(((bf16[1,84,512]{2,1,0:T(8,128)(2,1)}), bf16[64,84,512]{2,1,0:T(8,128)(2,1)}) %all-gather.18.cloned.1.call-update) | async-done | bytes 5505040 | tf_op jit(solution)/shard_map/all_gather | solution.py:118
  730.3 8.9 %reshape.185 = bf16[5376,512]{1,0:T(8,128)(2,1)} reshape(bf16[64,84,512]{2,1,0:T(8,128)(2,1)} %all-gather.18.cloned.1.call-done) | data formatting | bytes 11010048
  739.2 5.7 convolution_convert_fusion
  744.9 0.0 reduce-scatter.2.cloned.1.call-update
  744.9 0.8 dynamic_slice.11
  745.7 40.0 %reduce-scatter.2.cloned.1.call-done = bf16[256,672]{0,1:T(8,128)(2,1)} async-done(((bf16[256,5376]{0,1:T(8,128)(2,1)}), bf16[256,672]{0,1:T(8,128)(2,1)}) %reduce-scatter.2.cloned.1.call-update) | async-done | bytes 344080 | tf_op jit(solution)/shard_map/reduce_scatter | solution.py:121
  785.7 1.1 fusion.27
  786.8 15.2 %psum.7 = f32[256]{0:T(256)S(1)} all-reduce(f32[256]{0:T(256)S(1)} %fusion.27), channel_id=1, replica_groups=mesh['seq'=64,'tp'=8] {'tp'}, use_global_device_ids=true, to_apply=%region_7.8 | all-reduce | flops 256 | bytes 2048 | tf_op jit(solution)/shard_map/psum | solution.py:125
  802.1 1.9 fusion.30
  (30 shorter events, 0.3 us)
Async XLA Ops:
  6.5 52.0 %all-gather.10.cloned.1.call-start = ((), (), s32[]{:S(2)}) async-start(), calls=%async_computation.1 | async-start | bytes 3096576 | tf_op jit(solution)/shard_map/all_gather | solution.py:54
  7.3 200.2 %all-gather.14.cloned.1.call-start = ((), (), s32[]{:S(2)}) async-start(), calls=%async_computation.4 | async-start | bytes 2928640 | tf_op jit(solution)/shard_map/all_gather | solution.py:82
  8.0 343.5 %all-gather.12.cloned.1.call-start = ((), (), s32[]{:S(2)}) async-start(), calls=%async_computation.3 | async-start | bytes 2928640 | tf_op jit(solution)/shard_map/all_gather | solution.py:83
  8.7 549.2 %all-gather.16.cloned.1.call-start = ((), (), s32[]{:S(2)}) async-start(), calls=%async_computation.5 | async-start | bytes 5857280 | tf_op jit(solution)/shard_map/all_gather | solution.py:81
  9.3 721.0 %all-gather.18.cloned.1.call-start = ((), (), s32[]{:S(2)}) async-start(), calls=%async_computation.6 | async-start | bytes 5857280 | tf_op jit(solution)/shard_map/all_gather | solution.py:118
  9.9 775.8 %reduce-scatter.2.cloned.1.call-start = ((), (), s32[]{:S(2)}) async-start(), calls=%async_computation.2 | async-start | bytes 3096576 | tf_op jit(solution)/shard_map/reduce_scatter | solution.py:121
  12.1 200.6 %copy-start.9 = (f32[5376]{0:T(1024)S(1)}, f32[5376]{0:T(1024)}, u32[]{:S(2)}) copy-start(f32[5376]{0:T(1024)} %param.11) | copy-start | bytes 64516
  58.5 154.1 %copy-start = (bf16[256,5376]{0,1:T(8,128)(2,1)S(1)}, bf16[256,5376]{0,1:T(8,128)(2,1)}, u32[]{:S(2)}) copy-start(bf16[256,5376]{0,1:T(8,128)(2,1)} %all-gather.10.cloned.1.call-done) | copy-start | bytes 8257540
  61.2 155.0 %copy-start.5 = (f32[256]{0:T(256)}, f32[256]{0:T(256)S(1)}, u32[]{:S(2)}) copy-start(f32[256]{0:T(256)S(1)} %add_rsqrt_fusion.3) | copy-start | bytes 3076
  216.3 140.4 %copy-start.6 = (f32[256]{0:T(256)S(1)}, f32[256]{0:T(256)}, u32[]{:S(2)}) copy-start(f32[256]{0:T(256)} %copy-done.5) | copy-start | bytes 3076
  216.3 140.3 %copy-start.10 = (f32[5376]{0:T(1024)S(1)}, f32[5376]{0:T(1024)}, u32[]{:S(2)}) copy-start(f32[5376]{0:T(1024)} %param.11) | copy-start | bytes 64516
  360.2 16.2 %collective-permute-start = (bf16[2,256,256]{1,2,0:T(8,128)(2,1)S(1)}, bf16[2,256,256]{1,2,0:T(8,128)(2,1)S(1)}, u32[]{:S(2)}, u32[]{:S(2)}) collective-permute-start(bf16[2,256,256]{1,2,0:T(8,128)(2,1)S(1)} %pad_maximum_fusion.1), channel_id=1, source_target_pairs={{0,32},{8,40},{16,48},{24,56},{32,64},{40,72},{48,80},{56,88},{64,... | collective-permute-start | bytes 786440 | tf_op jit(solution)/shard_map/ppermute | solution.py:15
  364.4 12.1 %collective-permute-start.1 = (bf16[2,256,256]{1,2,0:T(8,128)(2,1)S(1)}, bf16[2,256,256]{1,2,0:T(8,128)(2,1)S(1)}, u32[]{:S(2)}, u32[]{:S(2)}) collective-permute-start(bf16[2,256,256]{1,2,0:T(8,128)(2,1)S(1)} %pad_maximum_fusion.1), channel_id=1, source_target_pairs={{0,24},{8,32},{16,40},{24,48},{32,56},{40,64},{48,72},{56,80},{64,... | collective-permute-start | bytes 786440 | tf_op jit(solution)/shard_map/ppermute | solution.py:15
  369.0 14.6 %collective-permute-start.2 = (bf16[2,256,256]{1,2,0:T(8,128)(2,1)S(1)}, bf16[2,256,256]{1,2,0:T(8,128)(2,1)S(1)}, u32[]{:S(2)}, u32[]{:S(2)}) collective-permute-start(bf16[2,256,256]{1,2,0:T(8,128)(2,1)S(1)} %pad_maximum_fusion.1), channel_id=1, source_target_pairs={{0,16},{8,24},{16,32},{24,40},{32,48},{40,56},{48,64},{56,72},{64,... | collective-permute-start | bytes 786440 | tf_op jit(solution)/shard_map/ppermute | solution.py:15
  373.5 14.8 %collective-permute-start.3 = (bf16[2,256,256]{1,2,0:T(8,128)(2,1)S(1)}, bf16[2,256,256]{1,2,0:T(8,128)(2,1)S(1)}, u32[]{:S(2)}, u32[]{:S(2)}) collective-permute-start(bf16[2,256,256]{1,2,0:T(8,128)(2,1)S(1)} %pad_maximum_fusion.1), channel_id=1, source_target_pairs={{0,8},{8,16},{16,24},{24,32},{32,40},{40,48},{48,56},{56,64},{64,7... | collective-permute-start | bytes 786440 | tf_op jit(solution)/shard_map/ppermute | solution.py:15
  389.4 177.4 %copy-start.7 = (f32[256]{0:T(256)S(1)}, f32[256]{0:T(256)}, u32[]{:S(2)}) copy-start(f32[256]{0:T(256)} %copy-done.5) | copy-start | bytes 3076
  566.8 8.2 %copy-start.8 = (f32[128]{0:T(128)S(1)}, f32[128]{0:T(128)}, u32[]{:S(2)}) copy-start(f32[128]{0:T(128)} %param.15) | copy-start | bytes 1540
  573.3 2.6 copy-start.4
  573.3 3.1 copy-start.3
  576.5 1.6 copy-start.2
  739.2 62.9 %copy-start.1 = (bf16[256,672]{0,1:T(8,128)(2,1)S(1)}, bf16[256,672]{0,1:T(8,128)(2,1)}, u32[]{:S(2)}) copy-start(bf16[256,672]{0,1:T(8,128)(2,1)} %param.10) | copy-start | bytes 1032196
Sparse Core Ops, SparseCore 0:
  9.4 49.0 all-gather.9
  63.1 144.3 all-gather.13
  212.1 139.3 all-gather.11
  355.9 201.9 all-gather.15
  562.2 167.9 all-gather.17
  745.0 40.6 reduce-scatter.1
where the time goes:
time: 812 us; the launch traced here: 811 us
  waiting for transfers between devices  701 us (86%)
  local copies, waits for them, and re-layouts  32.4 us (4%)
  matrix products  22.3 us (3%)
  blocking collectives  15.2 us (2%)
  starting transfers between devices  14.8 us (2%)
  between operations  13.8 us (2%)
  other arithmetic  10.9 us (1%)
    all_gather x1, waiting for transfers between devices, local(): lax.all_gather(w_query, 'seq', axis=0, tiled=True)  169 us
    all_gather x1, waiting for transfers between devices, local(): lax.all_gather(w_out, 'seq', axis=1, tiled=True)  151 us
    all_gather x1, waiting for transfers between devices, local(): lax.all_gather(key_weight, 'seq', axis=0, tiled=True)  146 us
    all_gather x1, waiting for transfers between devices, local(): lax.all_gather(value_weight, 'seq', axis=0, tiled=True)  134 us
    all_gather x1, waiting for transfers between devices, local(): gathered = lax.all_gather(residual, 'tp', axis=1, tiled=True)  46.5 us
    reduce_scatter x1, waiting for transfers between devices, local(): lax.psum_scatter(partial_out.astype(jnp.bfloat16), 'tp', scatter_dimensio...  40 us
    unnamed x29, local copies, waits for them, and re-layouts  28.2 us
  transfers between devices with their start and end apart: 10, of which 8 were waited for; matrix products, arithmetic and copies ran while one was open for 6% of the time, Pallas kernels for 0%

commit v1 on v0

--- a/solution.py
+++ b/solution.py
@@ -2,6 +2,7 @@
 import jax.numpy as jnp
 from jax import lax
 from jax.sharding import PartitionSpec as P
+from jax.lax import all_to_all, axis_size
 
 LOOKBACK_SPAN = 1024
 epsilon = 1e-06
@@ -77,10 +78,13 @@
         )
         return (total, summed)
 
+    tell_chains_for = lambda w_in, shard_axis, pos_dim: jnp.concatenate(
+        all_to_all(jnp.stack(axis_size(shard_axis) * [w_in], 0), shard_axis, 0, 0), pos_dim
+    )
     pieces = (
         lax.all_gather(w_query, "seq", axis=0, tiled=True),
         lax.all_gather(key_weight, "seq", axis=0, tiled=True),
-        lax.all_gather(value_weight, "seq", axis=0, tiled=True),
+        tell_chains_for(value_weight, "seq", 0),
     )
     queries_raw, unrotated_keys, projected_values = tuple(
         (jnp.dot(normalized_input, piece, preferred_element_type=jnp.float32) for piece in pieces)

time: 812 us -> 702 us (0.86)
  the two profiles are of different devices: /device:TPU:8 before, /device:TPU:2 now
where the time goes in v1:
time: 702 us; the launch traced here: 700 us
  waiting for transfers between devices  572 us (81%)
  starting transfers between devices  33.3 us (5%)
  local copies, waits for them, and re-layouts  32.3 us (5%)
  matrix products  24.7 us (4%)
  blocking collectives  15.1 us (2%)
  between operations  13.5 us (2%)
  other arithmetic  9.41 us (1%)
    all_gather x1, waiting for transfers between devices, local(): lax.all_gather(w_out, 'seq', axis=1, tiled=True)  151 us
    all_gather x1, waiting for transfers between devices, local(): lax.all_gather(key_weight, 'seq', axis=0, tiled=True)  147 us
    all_gather x1, waiting for transfers between devices, local(): lax.all_gather(w_query, 'seq', axis=0, tiled=True)  138 us
    all_gather x1, waiting for transfers between devices, local(): gathered = lax.all_gather(residual, 'tp', axis=1, tiled=True)  89 us
    reduce_scatter x1, waiting for transfers between devices, local(): lax.psum_scatter(partial_out.astype(jnp.bfloat16), 'tp', scatter_dimensio...  39.8 us
    unnamed x24, local copies, waits for them, and re-layouts  23 us
    all_to_all x1, starting transfers between devices, local(): all_to_all(jnp.stack(axis_size(shard_axis) * [w_in], 0), shard_axis, 0, 0)  19.1 us
    dot_general x3, matrix products, local(): jnp.dot(normalized_input, piece, preferred_element_type=jnp.float32)  15.9 us
  transfers between devices with their start and end apart: 10, of which 6 were waited for; matrix products, arithmetic and copies ran while one was open for 7% of the time, Pallas kernels for 0%

profile of v1, /device:TPU:2, one launch (start us, length us, event | category | flops | bytes accessed | tf_op | source)
XLA Modules:
  0.0 700.5 jit_solution(4153090253099060304)
XLA Ops:
  6.5 0.0 all-gather.8.cloned.1.call-start
  6.5 0.7 all-gather.8.cloned.1.call-update
  7.3 0.0 all-gather.10.cloned.1.call-start
  7.3 0.7 all-gather.10.cloned.1.call-update
  8.0 0.0 all-gather.12.cloned.1.call-start
  8.1 0.7 all-gather.12.cloned.1.call-update
  8.7 0.0 all-gather.14.cloned.1.call-start
  8.8 0.5 all-gather.14.cloned.1.call-update
  9.3 0.0 copy-start.4
  9.3 2.5 stack.8
  11.9 19.1 %all-to-all-start = ((bf16[64,84,256]{2,1,0:T(8,128)(2,1)}), bf16[64,84,256]{2,1,0:T(8,128)(2,1)S(1)}, u32[]{:S(2)}, u32[]{:S(2)}) async-start(bf16[64,84,256]{2,1,0:T(8,128)(2,1)} %stack.8), calls=%async_computation | async-start | bytes 5767168 | tf_op jit(solution)/shard_map/all_to_all | solution.py:82
  31.0 0.0 reduce-scatter.2.cloned.1.call-start
  31.1 0.0 copy-done.4
  31.1 0.1 fusion.45
  31.2 0.1 pad_dynamic-slice_fusion
  31.2 0.5 multiply_cosine_fusion
  31.8 0.0 copy-start.8
  31.8 89.0 %all-gather.8.cloned.1.call-done = bf16[256,5376]{0,1:T(8,128)(2,1)} async-done(((bf16[256,672]{0,1:T(8,128)(2,1)}), bf16[256,5376]{0,1:T(8,128)(2,1)}) %all-gather.8.cloned.1.call-update) | async-done | bytes 2752528 | tf_op jit(solution)/shard_map/all_gather | solution.py:55
  120.8 2.5 fusion
  123.3 147.3 %all-gather.10.cloned.1.call-done = bf16[64,84,256]{2,1,0:T(8,128)(2,1)} async-done(((bf16[1,84,256]{2,1,0:T(8,128)(2,1)}), bf16[64,84,256]{2,1,0:T(8,128)(2,1)}) %all-gather.10.cloned.1.call-update) | async-done | bytes 2752528 | tf_op jit(solution)/shard_map/all_gather | solution.py:86
  270.6 5.2 reshape.185
  275.8 0.0 copy-done.8
  275.8 5.0 multiply_reduce_fusion.1
  280.8 1.1 copy.40
  281.9 0.1 multiply_multiply_fusion.1
  282.0 0.2 subtract_convert_fusion.1
  282.2 0.1 pad_maximum_fusion.2
  282.3 0.1 copy.46
  282.4 0.0 all-to-all-done
  282.5 2.3 reshape.180
  284.7 4.3 convolution_convert_fusion.1
  289.1 2.6 collective-permute-start
  291.7 0.8 fusion.20
  292.5 3.3 collective-permute-start.1
  295.8 4.3 collective-permute-start.2
  300.1 0.8 fusion.33
  300.8 3.9 collective-permute-start.3
  304.7 0.0 collective-permute-done
  304.8 0.0 collective-permute-done.1
  304.8 0.0 collective-permute-done.2
  304.8 4.3 collective-permute-done.3
  309.2 1.1 fusion.46
  310.3 137.9 %all-gather.12.cloned.1.call-done = bf16[64,84,512]{2,1,0:T(8,128)(2,1)} async-done(((bf16[1,84,512]{2,1,0:T(8,128)(2,1)}), bf16[64,84,512]{2,1,0:T(8,128)(2,1)}) %all-gather.12.cloned.1.call-update) | async-done | bytes 5505040 | tf_op jit(solution)/shard_map/all_gather | solution.py:85
  448.2 8.9 %reshape.187 = bf16[5376,512]{1,0:T(8,128)(2,1)} reshape(bf16[64,84,512]{2,1,0:T(8,128)(2,1)} %all-gather.12.cloned.1.call-done) | data formatting | bytes 11010048
  457.1 6.6 fusion.40
  463.6 1.3 reshape.182
  464.9 0.3 multiply_reduce_fusion
  465.3 0.3 multiply_multiply_fusion
  465.6 0.5 subtract_convert_fusion
  466.2 0.5 fusion.47
  466.7 0.0 copy-start.2
  466.8 0.0 copy-done.3
  466.8 1.3 fusion.3
  468.1 0.2 fusion.31
  468.4 0.9 fusion.24
  469.3 151.2 %all-gather.14.cloned.1.call-done = bf16[64,84,512]{2,1,0:T(8,128)(2,1)} async-done(((bf16[1,84,512]{2,1,0:T(8,128)(2,1)}), bf16[64,84,512]{2,1,0:T(8,128)(2,1)}) %all-gather.14.cloned.1.call-update) | async-done | bytes 5505040 | tf_op jit(solution)/shard_map/all_gather | solution.py:122
  620.6 8.9 %reshape.189 = bf16[5376,512]{1,0:T(8,128)(2,1)} reshape(bf16[64,84,512]{2,1,0:T(8,128)(2,1)} %all-gather.14.cloned.1.call-done) | data formatting | bytes 11010048
  629.5 5.7 convolution_convert_fusion
  635.2 0.0 reduce-scatter.2.cloned.1.call-update
  635.2 0.8 dynamic_slice.11
  636.0 39.8 %reduce-scatter.2.cloned.1.call-done = bf16[256,672]{0,1:T(8,128)(2,1)} async-done(((bf16[256,5376]{0,1:T(8,128)(2,1)}), bf16[256,672]{0,1:T(8,128)(2,1)}) %reduce-scatter.2.cloned.1.call-update) | async-done | bytes 344080 | tf_op jit(solution)/shard_map/reduce_scatter | solution.py:125
  675.8 1.1 fusion.27
  676.9 15.1 %psum.7 = f32[256]{0:T(256)S(1)} all-reduce(f32[256]{0:T(256)S(1)} %fusion.27), channel_id=1, replica_groups=mesh['seq'=64,'tp'=8] {'tp'}, use_global_device_ids=true, to_apply=%region_7.8 | all-reduce | flops 256 | bytes 2048 | tf_op jit(solution)/shard_map/psum | solution.py:129
  692.0 1.9 fusion.30
  (26 shorter events, 0.3 us)
Async XLA Ops:
  6.5 114.2 %all-gather.8.cloned.1.call-start = ((), (), s32[]{:S(2)}) async-start(), calls=%async_computation.2 | async-start | bytes 3096576 | tf_op jit(solution)/shard_map/all_gather | solution.py:55
  7.3 263.3 %all-gather.10.cloned.1.call-start = ((), (), s32[]{:S(2)}) async-start(), calls=%async_computation.4 | async-start | bytes 2928640 | tf_op jit(solution)/shard_map/all_gather | solution.py:86
  8.0 440.2 %all-gather.12.cloned.1.call-start = ((), (), s32[]{:S(2)}) async-start(), calls=%async_computation.5 | async-start | bytes 5857280 | tf_op jit(solution)/shard_map/all_gather | solution.py:85
  8.7 611.8 %all-gather.14.cloned.1.call-start = ((), (), s32[]{:S(2)}) async-start(), calls=%async_computation.6 | async-start | bytes 5857280 | tf_op jit(solution)/shard_map/all_gather | solution.py:122
  9.3 21.7 %copy-start.4 = (s32[16384]{0:T(1024)S(1)}, s32[16384]{0:T(1024)}, u32[]{:S(2)}) copy-start(s32[16384]{0:T(1024)} %param.19) | copy-start | bytes 196612
  11.9 270.6 %all-to-all-start = ((bf16[64,84,256]{2,1,0:T(8,128)(2,1)}), bf16[64,84,256]{2,1,0:T(8,128)(2,1)S(1)}, u32[]{:S(2)}, u32[]{:S(2)}) async-start(bf16[64,84,256]{2,1,0:T(8,128)(2,1)} %stack.8), calls=%async_computation | async-start | bytes 5767168 | tf_op jit(solution)/shard_map/all_to_all | solution.py:82
  31.0 644.8 %reduce-scatter.2.cloned.1.call-start = ((), (), s32[]{:S(2)}) async-start(), calls=%async_computation.3 | async-start | bytes 3096576 | tf_op jit(solution)/shard_map/reduce_scatter | solution.py:125
  31.8 244.0 %copy-start.8 = (f32[5376]{0:T(1024)S(1)}, f32[5376]{0:T(1024)}, u32[]{:S(2)}) copy-start(f32[5376]{0:T(1024)} %param.11) | copy-start | bytes 64516
  275.8 6.1 copy-start.6
  289.1 15.6 %collective-permute-start = (bf16[2,256,256]{1,2,0:T(8,128)(2,1)S(1)}, bf16[2,256,256]{1,2,0:T(8,128)(2,1)S(1)}, u32[]{:S(2)}, u32[]{:S(2)}) collective-permute-start(bf16[2,256,256]{1,2,0:T(8,128)(2,1)S(1)} %pad_maximum_fusion.1), channel_id=1, source_target_pairs={{0,32},{8,40},{16,48},{24,56},{32,64},{40,72},{48,80},{56,88},{64,... | collective-permute-start | bytes 786440 | tf_op jit(solution)/shard_map/ppermute | solution.py:16
  292.5 12.3 %collective-permute-start.1 = (bf16[2,256,256]{1,2,0:T(8,128)(2,1)S(1)}, bf16[2,256,256]{1,2,0:T(8,128)(2,1)S(1)}, u32[]{:S(2)}, u32[]{:S(2)}) collective-permute-start(bf16[2,256,256]{1,2,0:T(8,128)(2,1)S(1)} %pad_maximum_fusion.1), channel_id=1, source_target_pairs={{0,24},{8,32},{16,40},{24,48},{32,56},{40,64},{48,72},{56,80},{64,... | collective-permute-start | bytes 786440 | tf_op jit(solution)/shard_map/ppermute | solution.py:16
  295.8 9.0 %collective-permute-start.2 = (bf16[2,256,256]{1,2,0:T(8,128)(2,1)S(1)}, bf16[2,256,256]{1,2,0:T(8,128)(2,1)S(1)}, u32[]{:S(2)}, u32[]{:S(2)}) collective-permute-start(bf16[2,256,256]{1,2,0:T(8,128)(2,1)S(1)} %pad_maximum_fusion.1), channel_id=1, source_target_pairs={{0,16},{8,24},{16,32},{24,40},{32,48},{40,56},{48,64},{56,72},{64,... | collective-permute-start | bytes 786440 | tf_op jit(solution)/shard_map/ppermute | solution.py:16
  300.8 8.3 %collective-permute-start.3 = (bf16[2,256,256]{1,2,0:T(8,128)(2,1)S(1)}, bf16[2,256,256]{1,2,0:T(8,128)(2,1)S(1)}, u32[]{:S(2)}, u32[]{:S(2)}) collective-permute-start(bf16[2,256,256]{1,2,0:T(8,128)(2,1)S(1)} %pad_maximum_fusion.1), channel_id=1, source_target_pairs={{0,8},{8,16},{16,24},{24,32},{32,40},{40,48},{48,56},{56,64},{64,7... | collective-permute-start | bytes 786440 | tf_op jit(solution)/shard_map/ppermute | solution.py:16
  310.3 146.8 %copy-start = (bf16[256,5376]{0,1:T(8,128)(2,1)S(1)}, bf16[256,5376]{0,1:T(8,128)(2,1)}, u32[]{:S(2)}) copy-start(bf16[256,5376]{0,1:T(8,128)(2,1)} %all-gather.8.cloned.1.call-done) | copy-start | bytes 8257540
  457.1 8.2 %copy-start.7 = (f32[128]{0:T(128)S(1)}, f32[128]{0:T(128)}, u32[]{:S(2)}) copy-start(f32[128]{0:T(128)} %param.15) | copy-start | bytes 1540
  463.6 2.6 copy-start.5
  463.6 3.1 copy-start.3
  466.7 1.6 copy-start.2
  629.5 62.6 %copy-start.1 = (bf16[256,672]{0,1:T(8,128)(2,1)S(1)}, bf16[256,672]{0,1:T(8,128)(2,1)}, u32[]{:S(2)}) copy-start(bf16[256,672]{0,1:T(8,128)(2,1)} %param.10) | copy-start | bytes 1032196
Sparse Core Ops, SparseCore 0:
  9.4 111.2 all-gather.7
  125.3 145.2 all-gather.9
  275.1 173.0 all-gather.11
  452.5 167.9 all-gather.13
  635.3 40.3 reduce-scatter.1
